TPU v7x, 256 devices: a whole 4x4x8 slice. The times are simulated.
256 devices in a mesh: lat: 8 (over y, z_lo), lon: 8 (over x, core), dp: 4 (over z_hi).
Axes of the slice: x: 4, y: 4, z: 8 (z_hi: 4, z_lo: 2; z = z_hi * 2 + z_lo), core: 2. Of those that a mesh axis runs over, the one named last changes fastest.
Arguments:
- state_grid: bfloat16 [4, 384, 768, 128], P('dp', ('lat', 'lon')), may hold values from -6 to 6
- cotangent: bfloat16 [4, 384, 768, 128], P('dp', ('lat', 'lon')), may hold values from -6 to 6
- legendre: bfloat16 [384, 384, 384], P(('lat', 'lon')), may hold values from -0.3125 to 0.3125
- wave_ids: int32 [384], replicated, may hold values from 0 to 383, each once
- weights: bfloat16 [384, 2, 4, 1024], P('lat'), may hold values from -0.75 to 0.75
Outputs:
- input_grad: bfloat16 [4, 384, 768, 128], P('dp', ('lat', 'lon'))
- weight_grad: float32 [384, 2, 4, 1024], P('lat')
Inputs may be any that keep to these rules, and one draw needn't show every extreme that they name: wave_ids[j] is the wavenumber of slot j; each of 0 to 383 stands in exactly one slot.
All inputs are finite; a program needn't handle non-finite values.
Results may differ from a plain program's by a relative error of at most 0.034.
Values may be sent and summed in bfloat16 or wider, within the bound.
No kernel may reach another device: no remote copies, remote signals or barrier semaphores. Data moves between devices by JAX's collectives and lax.ppermute only.
A program may use at most 128 MiB of HBM per device.

v0:
```python
import math
import jax
import jax.numpy as jnp
from jax import lax
from jax.sharding import PartitionSpec as P

NLON = 768
GROUPS = 4
GROUP_WIDTH = 32


def build_tables(wave_ids):
    columns = jnp.arange(NLON, dtype=jnp.int32)
    phase_int = wave_ids[:, None] * columns[None, :] % NLON
    angles = phase_int.astype(jnp.float32) * jnp.float32(2.0 * math.pi / NLON)
    factor = jnp.float32(1.0 / math.sqrt(NLON))
    paired = jnp.stack([jnp.cos(angles) * factor, -jnp.sin(angles) * factor], axis=1)
    forward_table = paired.reshape(2 * wave_ids.shape[0], NLON)
    doubling = jnp.where(wave_ids == 0, 1.0, 2.0).astype(jnp.float32)
    inverse_table = forward_table * jnp.repeat(doubling, 2)[:, None]
    return (forward_table.astype(jnp.bfloat16), inverse_table.astype(jnp.bfloat16))


def build_kernel(weights):
    degree_count = weights.shape[0]
    real_part = weights[:, 0].reshape(degree_count, GROUPS, GROUP_WIDTH, GROUP_WIDTH)
    imag_part = weights[:, 1].reshape(degree_count, GROUPS, GROUP_WIDTH, GROUP_WIDTH)
    upper_rows = jnp.stack([real_part, imag_part], axis=3)
    lower_rows = jnp.stack([-imag_part, real_part], axis=3)
    return jnp.stack([upper_rows, lower_rows], axis=2)


def gelu_slope(branch):
    normal_cdf = 0.5 * (1.0 + lax.erf(branch * (1.0 / math.sqrt(2.0))))
    density = jnp.exp(-0.5 * branch * branch) * (1.0 / math.sqrt(2.0 * math.pi))
    return normal_cdf + branch * density


def shards(state_grid, cotangent, legendre, wave_ids, weights):
    lat_count = lax.axis_size("lat")
    lon_count = lax.axis_size("lon")
    samples, rows_dev, lon_cells, channels = state_grid.shape
    slot_count, lat_cells, degree_count = legendre.shape
    slot_reals = 2 * slot_count
    first_slot = (lax.axis_index("lat") * lon_count + lax.axis_index("lon")) * slot_count
    held_waves = lax.dynamic_slice_in_dim(wave_ids, first_slot, slot_count)
    degree_ids = jnp.arange(degree_count, dtype=jnp.int32)
    masked = jnp.where(
        degree_ids[None, None, :] >= held_waves[:, None, None],
        legendre,
        jnp.zeros((), legendre.dtype),
    )
    slot_order = wave_ids.reshape(lat_count, lon_count, slot_count).transpose(1, 0, 2).reshape(-1)
    forward_table, inverse_table = build_tables(slot_order)
    kernel = build_kernel(weights)

    def analyze(source, twiddle):
        spectra = jnp.einsum(
            "srnc,kn->srkc", source, twiddle, preferred_element_type=jnp.float32
        ).astype(jnp.bfloat16)
        gathered = lax.all_to_all(
            lax.all_to_all(spectra, "lon", split_axis=2, concat_axis=1, tiled=True),
            "lat",
            split_axis=2,
            concat_axis=1,
            tiled=True,
        )
        blocks = gathered.reshape(samples, lat_cells, slot_count, 2 * channels)
        spectral = jnp.einsum("samc,mal->slmc", blocks, masked, preferred_element_type=jnp.float32)
        spectral = spectral.astype(jnp.bfloat16).reshape(
            samples, degree_count, slot_reals, channels
        )
        return lax.all_to_all(spectral, "lat", split_axis=1, concat_axis=2, tiled=True)

    def synthesize(spectral, twiddle):
        joined = lax.all_to_all(spectral, "lat", split_axis=2, concat_axis=1, tiled=True)
        blocks = joined.reshape(samples, degree_count, slot_count, 2 * channels)
        spectra = jnp.einsum(
            "slmc,mal->samc", blocks, masked, preferred_element_type=jnp.float32
        ).astype(jnp.bfloat16)
        spectra = spectra.reshape(samples, lat_cells, slot_reals, channels)
        pencil = lax.all_to_all(
            lax.all_to_all(spectra, "lat", split_axis=1, concat_axis=2, tiled=True),
            "lon",
            split_axis=1,
            concat_axis=2,
            tiled=True,
        )
        return jnp.einsum("srkc,kn->srnc", pencil, twiddle, preferred_element_type=jnp.float32)

    def split_groups(spectral):
        return spectral.reshape(samples, spectral.shape[1], -1, 2, GROUPS, GROUP_WIDTH)

    coef_fwd = analyze(state_grid, forward_table)
    coef_six = split_groups(coef_fwd)
    mixed_coef = jnp.einsum(
        "slmpgi,lgpiqo->slmqgo", coef_six, kernel, preferred_element_type=jnp.float32
    ).astype(jnp.bfloat16)
    branch = synthesize(mixed_coef.reshape(coef_fwd.shape), inverse_table)
    pulled = (cotangent.astype(jnp.float32) * gelu_slope(branch)).astype(jnp.bfloat16)
    back_coef = analyze(pulled, inverse_table)
    back_six = split_groups(back_coef)
    outer_sums = jnp.einsum(
        "slmpgi,slmqgo->lgpiqo", coef_six, back_six, preferred_element_type=jnp.float32
    )
    real_grad = outer_sums[:, :, 0, :, 0, :] + outer_sums[:, :, 1, :, 1, :]
    imag_grad = outer_sums[:, :, 0, :, 1, :] - outer_sums[:, :, 1, :, 0, :]
    local_grad = jnp.stack([real_grad, imag_grad], axis=1).reshape(weights.shape)
    weight_grad = lax.psum(local_grad.astype(jnp.bfloat16), ("lon", "dp")).astype(jnp.float32)
    demixed = jnp.einsum(
        "slmqgo,lgpiqo->slmpgi", back_six, kernel, preferred_element_type=jnp.float32
    ).astype(jnp.bfloat16)
    returned = synthesize(demixed.reshape(back_coef.shape), forward_table)
    input_grad = (cotangent.astype(jnp.float32) + returned).astype(jnp.bfloat16)
    return (input_grad, weight_grad)


def solution(mesh):
    return jax.shard_map(
        shards,
        mesh=mesh,
        in_specs=(
            P("dp", ("lat", "lon"), None, None),
            P("dp", ("lat", "lon"), None, None),
            P(("lat", "lon"), None, None),
            P(),
            P("lat", None, None, None),
        ),
        out_specs=(P("dp", ("lat", "lon"), None, None), P("lat", None, None, None)),
        check_vma=False,
    )
```

profile of v0, /device:TPU:8, one launch (start us, length us, event | category | flops | bytes accessed | tf_op | source)
XLA Modules:
  0.0 725.3 jit_solution(13457028617643623277)
XLA Ops:
  8.2 4.9 cosine_multiply_fusion
  13.3 2.2 copy.215
  15.6 3.7 reshape.366
  19.3 2.4 fusion.14
  22.5 25.9 %all_to_all.192 = bf16[1,6,768,128]{3,1,0,2:T(8,128)(2,1)S(1)} all-to-all(bf16[1,6,768,128]{3,1,0,2:T(8,128)(2,1)S(1)} %copy.223), channel_id=1, replica_groups=mesh['lat'=8,'lon'=8,'dp'=4] {'lon'}, dimensions={2} | all-to-all | bytes 2359296 | tf_op jit(solution)/shard_map/all_to_all | solution.py:62
  48.7 1.5 copy.226
  50.1 6.5 all-to-all-start.1
  57.4 13.8 %all-to-all-done.1 = bf16[1,48,96,128]{3,1,0,2:T(8,128)(2,1)S(1)} async-done(((bf16[1,48,96,128]{3,1,0,2:T(8,128)(2,1)}), bf16[1,48,96,128]{3,1,0,2:T(8,128)(2,1)S(1)}, u32[]{:S(2)}, u32[]{:S(2)}) %all-to-all-start.1) | async-done | bytes 1179680 | tf_op jit(solution)/shard_map/all_to_all | solution.py:61
  71.2 3.0 copy.280
  74.2 4.4 reshape.378
  78.7 3.4 convolution_convert_fusion.1
  82.1 2.9 copy.229
  85.0 6.4 all-to-all-start.2
  92.5 1.6 copy.298
  95.3 2.2 copy.299
  97.5 2.7 maximum_bitcast_fusion
  100.2 3.0 pad_maximum_fusion
  103.2 12.7 %copy.232 = bf16[48,4,2,32,2,32]{3,5,2,4,1,0:T(8,128)(2,1)} copy(bf16[48,4,2,32,2,32]{0,5,4,3,1,2:T(8,128)(2,1)} %pad_maximum_fusion) | data formatting | bytes 3145728 | tf_op jit(solution)/shard_map/stack | solution.py:30
  115.8 1.7 copy.230
  117.6 2.7 copy.231
  120.3 8.3 %copy.270 = bf16[48,48,2,4,32,1]{1,4,2,5,3,0:T(8,128)(2,1)} copy(bf16[48,48,2,4,32,1]{0,4,3,2,1,5:T(8,128)(2,1)} %bitcast.179) | data formatting | bytes 2359296 | tf_op jit(solution)/shard_map/reshape.8
  128.5 6.7 fusion
  135.3 8.3 %copy.234 = bf16[1,48,48,2,4,32]{1,5,4,3,2,0:T(8,128)(2,1)} copy(bf16[1,48,48,2,4,32]{2,5,3,4,1,0:T(8,128)(2,1)} %fusion) | data formatting | bytes 2359296 | tf_op jit(solution)/shard_map/convert_element_type | solution.py:98
  143.5 3.2 copy.235
  146.7 19.4 %all_to_all.193 = bf16[1,48,96,128]{3,1,0,2:T(8,128)(2,1)} all-to-all(bf16[1,48,96,128]{3,1,0,2:T(8,128)(2,1)S(1)} %copy.235), channel_id=1, replica_groups=mesh['lat'=8,'lon'=8,'dp'=4] {'lat'}, dimensions={2} | all-to-all | bytes 2359296 | tf_op jit(solution)/shard_map/all_to_all | solution.py:76
  166.2 4.2 copy.283
  170.4 4.4 reshape.379
  174.8 3.5 convolution_convert_fusion.3
  178.3 2.9 copy.238
  181.2 21.5 %all_to_all.194 = bf16[1,384,12,128]{3,2,0,1:T(8,128)(2,1)S(1)} all-to-all(bf16[1,384,12,128]{3,2,0,1:T(8,128)(2,1)} %copy.238), channel_id=1, replica_groups=mesh['lat'=8,'lon'=8,'dp'=4] {'lat'}, dimensions={1} | all-to-all | bytes 2359296 | tf_op jit(solution)/shard_map/all_to_all | solution.py:83
  204.4 4.3 all-to-all-start.5
  211.1 14.9 %all-to-all-done.5 = bf16[1,48,96,128]{3,2,0,1:T(8,128)(2,1)} async-done(((bf16[1,48,96,128]{3,2,0,1:T(8,128)(2,1)}), bf16[1,48,96,128]{3,2,0,1:T(8,128)(2,1)}, u32[]{:S(2)}, u32[]{:S(2)}) %all-to-all-start.5) | async-done | bytes 1179680 | tf_op jit(solution)/shard_map/all_to_all | solution.py:82
  227.4 4.8 fusion.15
  232.3 2.1 copy.244
  234.4 24.2 %all_to_all.195 = bf16[1,6,768,128]{3,1,0,2:T(8,128)(2,1)S(1)} all-to-all(bf16[1,6,768,128]{3,1,0,2:T(8,128)(2,1)S(1)} %copy.244), channel_id=1, replica_groups=mesh['lat'=8,'lon'=8,'dp'=4] {'lon'}, dimensions={2} | all-to-all | bytes 2359296 | tf_op jit(solution)/shard_map/all_to_all | solution.py:62
  259.3 20.1 %all_to_all.196 = bf16[1,48,96,128]{3,1,0,2:T(8,128)(2,1)S(1)} all-to-all(bf16[1,48,96,128]{3,1,0,2:T(8,128)(2,1)S(1)} %copy.247), channel_id=1, replica_groups=mesh['lat'=8,'lon'=8,'dp'=4] {'lat'}, dimensions={2} | all-to-all | bytes 2359296 | tf_op jit(solution)/shard_map/all_to_all | solution.py:61
  279.4 3.0 copy.284
  282.4 4.4 reshape.380
  286.8 2.4 convolution_convert_fusion
  289.2 2.0 copy.250
  291.1 5.1 all-to-all-start.8
  296.3 11.6 %copy.253 = bf16[48,4,2,32,2,32]{5,3,4,2,1,0:T(8,128)(2,1)} copy(bf16[48,4,2,32,2,32]{0,5,4,3,1,2:T(8,128)(2,1)} %pad_maximum_fusion) | data formatting | bytes 3145728 | tf_op jit(solution)/shard_map/stack | solution.py:30
  307.8 6.3 all-to-all-done.8
  314.5 2.7 copy.252
  317.2 8.3 %copy.273 = bf16[48,48,2,4,32,1]{1,4,2,5,3,0:T(8,128)(2,1)} copy(bf16[48,48,2,4,32,1]{0,4,3,2,1,5:T(8,128)(2,1)} %bitcast.182) | data formatting | bytes 2359296 | tf_op jit(solution)/shard_map/reshape.39
  325.5 6.8 fusion.1
  332.3 8.3 %copy.255 = bf16[1,48,48,2,4,32]{1,5,4,3,2,0:T(8,128)(2,1)} copy(bf16[1,48,48,2,4,32]{2,5,3,4,1,0:T(8,128)(2,1)} %fusion.1) | data formatting | bytes 2359296 | tf_op jit(solution)/shard_map/convert_element_type | solution.py:112
  340.6 3.2 copy.256
  343.8 19.7 %all_to_all.197 = bf16[1,48,96,128]{3,1,0,2:T(8,128)(2,1)S(1)} all-to-all(bf16[1,48,96,128]{3,1,0,2:T(8,128)(2,1)S(1)} %copy.256), channel_id=1, replica_groups=mesh['lat'=8,'lon'=8,'dp'=4] {'lat'}, dimensions={2} | all-to-all | bytes 2359296 | tf_op jit(solution)/shard_map/all_to_all | solution.py:76
  363.5 3.0 copy.287
  366.4 4.4 reshape.381
  370.9 2.4 convolution_convert_fusion.2
  373.3 2.0 copy.259
  375.3 5.3 all-to-all-start.10
  380.6 8.3 %copy.276 = bf16[48,48,2,4,32,1]{1,4,5,2,3,0:T(8,128)(2,1)} copy(bf16[48,48,2,4,32,1]{0,4,3,2,1,5:T(8,128)(2,1)} %bitcast.180) | data formatting | bytes 2359296 | tf_op jit(solution)/shard_map/reshape.8
  388.9 12.5 %fusion.41 = f32[48,4,2,32,2,32]{5,3,4,2,1,0:T(8,128)} fusion(bf16[48,48,2,4,32,1]{1,4,5,2,3,0:T(8,128)(2,1)} %copy.276, bf16[48,48,2,4,32,1]{1,4,2,5,3,0:T(8,128)(2,1)} %copy.273), kind=kOutput, calls=%fused_computation.66 | convolution fusion | flops 75497472 | bytes 5505024 | tf_op jit(solution)/shard_map/slmpgi,slmqgo->lgpiqo/dot_general | solution.py:103
  403.1 4.3 all-to-all-start.11
  407.4 7.5 %fusion.3 = (bf16[48,4,1,32,1,32]{5,3,4,2,1,0:T(8,128)(2,1)}, bf16[48,4,1,32,1,32]{5,3,4,2,1,0:T(8,128)(2,1)S(1)}) fusion(f32[48,4,2,32,2,32]{5,3,4,2,1,0:T(8,128)} %fusion.41), kind=kLoop, calls=%fused_computation.9 | loop fusion | flops 786432 | bytes 3932160 | tf_op jit(solution)/shard_map/convert.3
  415.0 2.9 reshape.382
  418.0 1.5 reshape.383
  421.6 290.0 %all-reduce.2.cloned.1.call-done = bf16[48,2,4,1024]{3,0,2,1:T(8,128)(2,1)} async-done(((bf16[48,2,4,1024]{3,0,2,1:T(8,128)(2,1)}), bf16[48,2,4,1024]{3,0,2,1:T(8,128)(2,1)}) %all-reduce.2.cloned.1.call-update) | async-done | bytes 786448 | tf_op jit(solution)/shard_map/psum | solution.py:109
  711.6 2.9 copy.269
  714.5 1.5 copy.263
  716.1 2.1 fusion.5
  (46 shorter events, 16.0 us)
Async XLA Ops:
  7.2 12.2 %copy-start = (bf16[1,6,768,128]{3,2,1,0:T(8,128)(2,1)S(1)}, bf16[1,6,768,128]{3,2,1,0:T(8,128)(2,1)}, u32[]{:S(2)}) copy-start(bf16[1,6,768,128]{3,2,1,0:T(8,128)(2,1)} %param.5) | copy-start | bytes 3538948
  50.1 21.1 %all-to-all-start.1 = ((bf16[1,48,96,128]{3,1,0,2:T(8,128)(2,1)}), bf16[1,48,96,128]{3,1,0,2:T(8,128)(2,1)S(1)}, u32[]{:S(2)}, u32[]{:S(2)}) async-start(bf16[1,48,96,128]{3,1,0,2:T(8,128)(2,1)} %copy.226), calls=%async_computation.1 | async-start | bytes 2359296 | tf_op jit(solution)/shard_map/all_to_all | solution.py:61
  85.0 6.4 copy-start.3
  85.0 30.9 %all-to-all-start.2 = ((bf16[1,384,12,128]{3,2,0,1:T(8,128)(2,1)}), bf16[1,384,12,128]{3,2,0,1:T(8,128)(2,1)}, u32[]{:S(2)}, u32[]{:S(2)}) async-start(bf16[1,384,12,128]{3,2,0,1:T(8,128)(2,1)} %copy.229), calls=%async_computation.2 | async-start | bytes 3145728 | tf_op jit(solution)/shard_map/all_to_all | solution.py:73
  204.4 21.6 %all-to-all-start.5 = ((bf16[1,48,96,128]{3,2,0,1:T(8,128)(2,1)}), bf16[1,48,96,128]{3,2,0,1:T(8,128)(2,1)}, u32[]{:S(2)}, u32[]{:S(2)}) async-start(bf16[1,48,96,128]{3,2,0,1:T(8,128)(2,1)} %copy.241), calls=%async_computation.5 | async-start | bytes 2359296 | tf_op jit(solution)/shard_map/all_to_all | solution.py:82
  291.1 23.0 %all-to-all-start.8 = ((bf16[1,384,12,128]{3,2,0,1:T(8,128)(2,1)}), bf16[1,384,12,128]{3,2,0,1:T(8,128)(2,1)S(1)}, u32[]{:S(2)}, u32[]{:S(2)}) async-start(bf16[1,384,12,128]{3,2,0,1:T(8,128)(2,1)} %copy.250), calls=%async_computation.8 | async-start | bytes 3145728 | tf_op jit(solution)/shard_map/all_to_all | solution.py:73
  375.3 26.1 %all-to-all-start.10 = ((bf16[1,384,12,128]{3,2,0,1:T(8,128)(2,1)}), bf16[1,384,12,128]{3,2,0,1:T(8,128)(2,1)S(1)}, u32[]{:S(2)}, u32[]{:S(2)}) async-start(bf16[1,384,12,128]{3,2,0,1:T(8,128)(2,1)} %copy.259), calls=%async_computation.10 | async-start | bytes 3145728 | tf_op jit(solution)/shard_map/all_to_all | solution.py:83
  403.1 311.3 %all-to-all-start.11 = ((bf16[1,48,96,128]{3,2,0,1:T(8,128)(2,1)}), bf16[1,48,96,128]{3,2,0,1:T(8,128)(2,1)}, u32[]{:S(2)}, u32[]{:S(2)}) async-start(bf16[1,48,96,128]{3,2,0,1:T(8,128)(2,1)} %copy.262), calls=%async_computation.11 | async-start | bytes 2359296 | tf_op jit(solution)/shard_map/all_to_all | solution.py:82
  407.4 304.2 %all-reduce.2.cloned.1.call-start = ((), (), s32[]{:S(2)}) async-start(), calls=%async_computation.12 | async-start | bytes 1572864 | tf_op jit(solution)/shard_map/psum | solution.py:109
  419.5 1.6 copy-start.2
  714.5 1.6 copy-start.4
  716.1 2.1 copy-start.1
Sparse Core Ops, SparseCore 0:
  420.8 290.7 all-reduce.1
where the time goes:
time: 735 us; the launch traced here: 725 us
  waiting for transfers between devices  325 us (44%)
  local copies, waits for them, and re-layouts  155 us (21%)
  blocking collectives  131 us (18%)
  matrix products  47 us (6%)
  starting transfers between devices  31.8 us (4%)
  other arithmetic  20.7 us (3%)
  between operations  14.6 us (2%)
    psum x1, waiting for transfers between devices, shards(): lax.psum(local_grad.astype(jnp.bfloat16), ('lon', 'dp')).astype(jnp.float32)  290 us
    another operation x11, local copies, waits for them, and re-layouts  55.7 us
    all_to_all x2, blocking collectives, analyze(): lax.all_to_all(spectra, 'lon', split_axis=2, concat_axis=1, tiled=True)  50.1 us
    all_to_all x2, blocking collectives, synthesize(): lax.all_to_all(spectral, 'lat', split_axis=2, concat_axis=1, tiled=True)  39.1 us
    another operation x2, local copies, waits for them, and re-layouts, build_kernel(): return jnp.stack([upper_rows, lower_rows], axis=2)  24.2 us
    all_to_all x1, blocking collectives, synthesize(): lax.all_to_all(spectra, 'lat', split_axis=1, concat_axis=2, tiled=True)  21.5 us
    all_to_all x1, blocking collectives, analyze(): lax.all_to_all(lax.all_to_all(spectra, 'lon', split_axis=2, concat_axis=1...  20.1 us
    all_to_all x2, waiting for transfers between devices, synthesize(): lax.all_to_all(lax.all_to_all(spectra, 'lat', split_axis=1, concat_axis=2...  14.9 us
  transfers between devices with their start and end apart: 7, of which 4 were waited for; matrix products, arithmetic and copies ran while one was open for 11% of the time, Pallas kernels for 0%

commit v1 on v0

--- a/solution.py
+++ b/solution.py
@@ -58,12 +58,20 @@
         spectra = jnp.einsum(
             "srnc,kn->srkc", source, twiddle, preferred_element_type=jnp.float32
         ).astype(jnp.bfloat16)
-        gathered = lax.all_to_all(
-            lax.all_to_all(spectra, "lon", split_axis=2, concat_axis=1, tiled=True),
-            "lat",
-            split_axis=2,
-            concat_axis=1,
-            tiled=True,
+        gathered = jnp.concatenate(
+            lax.all_to_all(
+                jnp.stack(
+                    jnp.split(
+                        lax.all_to_all(spectra, "lon", split_axis=2, concat_axis=1, tiled=True),
+                        lax.axis_size("lat"),
+                        axis=2,
+                    )
+                ),
+                "lat",
+                0,
+                0,
+            ),
+            axis=1,
         )
         blocks = gathered.reshape(samples, lat_cells, slot_count, 2 * channels)
         spectral = jnp.einsum("samc,mal->slmc", blocks, masked, preferred_element_type=jnp.float32)

time: 735 us -> 736 us (level)
    another operation x11 -> x15, local copies, waits for them, and re-layouts: 55.7 us -> 57.4 us
where the time goes in v1:
time: 736 us; the launch traced here: 726 us
  waiting for transfers between devices  325 us (44%)
  local copies, waits for them, and re-layouts  156 us (21%)
  blocking collectives  131 us (18%)
  matrix products  47 us (6%)
  starting transfers between devices  31.8 us (4%)
  other arithmetic  20.7 us (3%)
  between operations  14.6 us (2%)
    psum x1, waiting for transfers between devices, shards(): lax.psum(local_grad.astype(jnp.bfloat16), ('lon', 'dp')).astype(jnp.float32)  290 us
    another operation x11, local copies, waits for them, and re-layouts  55.7 us
    all_to_all x2, blocking collectives, analyze(): lax.all_to_all(spectra, 'lon', split_axis=2, concat_axis=1, tiled=True)  50.1 us
    all_to_all x2, blocking collectives, synthesize(): lax.all_to_all(spectral, 'lat', split_axis=2, concat_axis=1, tiled=True)  39.1 us
    another operation x2, local copies, waits for them, and re-layouts, build_kernel(): return jnp.stack([upper_rows, lower_rows], axis=2)  24.2 us
    all_to_all x1, blocking collectives, synthesize(): lax.all_to_all(spectra, 'lat', split_axis=1, concat_axis=2, tiled=True)  21.5 us
    all_to_all x1, blocking collectives, analyze(): lax.all_to_all(jnp.stack(jnp.split(lax.all_to_all(spectra, 'lon', split_a...  20.1 us
    all_to_all x2, waiting for transfers between devices, synthesize(): lax.all_to_all(lax.all_to_all(spectra, 'lat', split_axis=1, concat_axis=2...  14.9 us
  transfers between devices with their start and end apart: 7, of which 4 were waited for; matrix products, arithmetic and copies ran while one was open for 11% of the time, Pallas kernels for 0%

profile of v1, /device:TPU:8, one launch (start us, length us, event | category | flops | bytes accessed | tf_op | source)
XLA Modules:
  0.0 726.1 jit_solution(6526665762379113719)
XLA Ops:
  8.2 4.9 cosine_multiply_fusion
  13.3 2.2 copy.241
  15.6 3.7 reshape.362
  19.3 2.4 fusion.14
  22.5 25.9 %all_to_all.172 = bf16[1,6,768,128]{3,1,0,2:T(8,128)(2,1)S(1)} all-to-all(bf16[1,6,768,128]{3,1,0,2:T(8,128)(2,1)S(1)} %copy.249), channel_id=1, replica_groups=mesh['lat'=8,'lon'=8,'dp'=4] {'lon'}, dimensions={2} | all-to-all | bytes 2359296 | tf_op jit(solution)/shard_map/all_to_all | solution.py:65
  50.4 6.5 all-to-all-start.1
  57.8 13.8 %all-to-all-done.1 = bf16[8,1,48,12,128]{4,2,3,1,0:T(8,128)(2,1)S(1)} async-done(((bf16[8,1,48,12,128]{4,2,3,1,0:T(8,128)(2,1)}), bf16[8,1,48,12,128]{4,2,3,1,0:T(8,128)(2,1)S(1)}, u32[]{:S(2)}, u32[]{:S(2)}) %all-to-all-start.1) | async-done | bytes 1179680 | tf_op jit(solution)/shard_map/all_to_all | solution.py:62
  71.5 3.0 copy.311
  74.5 4.4 reshape.374
  79.0 3.4 convolution_convert_fusion.1
  82.4 2.9 copy.257
  85.3 6.4 all-to-all-start.2
  92.8 1.6 copy.330
  95.6 2.2 copy.331
  97.8 2.7 maximum_bitcast_fusion
  100.5 3.0 pad_maximum_fusion
  103.5 12.7 %copy.260 = bf16[48,4,2,32,2,32]{3,5,2,4,1,0:T(8,128)(2,1)} copy(bf16[48,4,2,32,2,32]{0,5,4,3,1,2:T(8,128)(2,1)} %pad_maximum_fusion) | data formatting | bytes 3145728 | tf_op jit(solution)/shard_map/stack | solution.py:30
  116.1 1.7 copy.258
  117.9 2.7 copy.259
  120.6 8.3 %copy.300 = bf16[48,48,2,4,32,1]{1,4,2,5,3,0:T(8,128)(2,1)} copy(bf16[48,48,2,4,32,1]{0,4,3,2,1,5:T(8,128)(2,1)} %bitcast.237) | data formatting | bytes 2359296 | tf_op jit(solution)/shard_map/reshape.7
  128.9 6.7 fusion
  135.6 8.3 %copy.262 = bf16[1,48,48,2,4,32]{1,5,4,3,2,0:T(8,128)(2,1)} copy(bf16[1,48,48,2,4,32]{2,5,3,4,1,0:T(8,128)(2,1)} %fusion) | data formatting | bytes 2359296 | tf_op jit(solution)/shard_map/convert_element_type | solution.py:106
  143.8 3.2 copy.263
  147.0 19.4 %all_to_all.173 = bf16[1,48,96,128]{3,1,0,2:T(8,128)(2,1)} all-to-all(bf16[1,48,96,128]{3,1,0,2:T(8,128)(2,1)S(1)} %copy.263), channel_id=1, replica_groups=mesh['lat'=8,'lon'=8,'dp'=4] {'lat'}, dimensions={2} | all-to-all | bytes 2359296 | tf_op jit(solution)/shard_map/all_to_all | solution.py:84
  166.5 4.2 copy.314
  170.7 4.4 reshape.375
  175.1 3.5 convolution_convert_fusion.3
  178.6 2.9 copy.266
  181.5 21.5 %all_to_all.174 = bf16[1,384,12,128]{3,2,0,1:T(8,128)(2,1)S(1)} all-to-all(bf16[1,384,12,128]{3,2,0,1:T(8,128)(2,1)} %copy.266), channel_id=1, replica_groups=mesh['lat'=8,'lon'=8,'dp'=4] {'lat'}, dimensions={1} | all-to-all | bytes 2359296 | tf_op jit(solution)/shard_map/all_to_all | solution.py:91
  204.7 4.3 all-to-all-start.5
  211.4 14.9 %all-to-all-done.5 = bf16[1,48,96,128]{3,2,0,1:T(8,128)(2,1)} async-done(((bf16[1,48,96,128]{3,2,0,1:T(8,128)(2,1)}), bf16[1,48,96,128]{3,2,0,1:T(8,128)(2,1)}, u32[]{:S(2)}, u32[]{:S(2)}) %all-to-all-start.5) | async-done | bytes 1179680 | tf_op jit(solution)/shard_map/all_to_all | solution.py:90
  226.4 1.4 copy.270
  227.7 4.8 fusion.15
  232.6 2.1 copy.272
  234.7 24.2 %all_to_all.175 = bf16[1,6,768,128]{3,1,0,2:T(8,128)(2,1)S(1)} all-to-all(bf16[1,6,768,128]{3,1,0,2:T(8,128)(2,1)S(1)} %copy.272), channel_id=1, replica_groups=mesh['lat'=8,'lon'=8,'dp'=4] {'lon'}, dimensions={2} | all-to-all | bytes 2359296 | tf_op jit(solution)/shard_map/all_to_all | solution.py:65
  259.9 20.1 %all_to_all.176 = bf16[8,1,48,12,128]{4,2,3,1,0:T(8,128)(2,1)S(1)} all-to-all(bf16[8,1,48,12,128]{4,2,3,1,0:T(8,128)(2,1)S(1)} %copy.277), channel_id=1, replica_groups=mesh['lat'=8,'lon'=8,'dp'=4] {'lat'}, dimensions={0} | all-to-all | bytes 2359296 | tf_op jit(solution)/shard_map/all_to_all | solution.py:62
  280.0 3.0 copy.316
  283.0 4.4 reshape.376
  287.4 2.4 convolution_convert_fusion
  289.8 2.0 copy.280
  291.8 5.1 all-to-all-start.8
  296.9 11.6 %copy.283 = bf16[48,4,2,32,2,32]{5,3,4,2,1,0:T(8,128)(2,1)} copy(bf16[48,4,2,32,2,32]{0,5,4,3,1,2:T(8,128)(2,1)} %pad_maximum_fusion) | data formatting | bytes 3145728 | tf_op jit(solution)/shard_map/stack | solution.py:30
  308.5 6.3 all-to-all-done.8
  315.1 2.7 copy.282
  317.8 8.3 %copy.303 = bf16[48,48,2,4,32,1]{1,4,2,5,3,0:T(8,128)(2,1)} copy(bf16[48,48,2,4,32,1]{0,4,3,2,1,5:T(8,128)(2,1)} %bitcast.240) | data formatting | bytes 2359296 | tf_op jit(solution)/shard_map/reshape.35
  326.1 6.8 fusion.1
  332.9 8.3 %copy.285 = bf16[1,48,48,2,4,32]{1,5,4,3,2,0:T(8,128)(2,1)} copy(bf16[1,48,48,2,4,32]{2,5,3,4,1,0:T(8,128)(2,1)} %fusion.1) | data formatting | bytes 2359296 | tf_op jit(solution)/shard_map/convert_element_type | solution.py:120
  341.2 3.2 copy.286
  344.4 19.7 %all_to_all.177 = bf16[1,48,96,128]{3,1,0,2:T(8,128)(2,1)S(1)} all-to-all(bf16[1,48,96,128]{3,1,0,2:T(8,128)(2,1)S(1)} %copy.286), channel_id=1, replica_groups=mesh['lat'=8,'lon'=8,'dp'=4] {'lat'}, dimensions={2} | all-to-all | bytes 2359296 | tf_op jit(solution)/shard_map/all_to_all | solution.py:84
  364.1 3.0 copy.319
  367.0 4.4 reshape.377
  371.5 2.4 convolution_convert_fusion.2
  373.9 2.0 copy.289
  375.9 5.3 all-to-all-start.10
  381.2 8.3 %copy.306 = bf16[48,48,2,4,32,1]{1,4,5,2,3,0:T(8,128)(2,1)} copy(bf16[48,48,2,4,32,1]{0,4,3,2,1,5:T(8,128)(2,1)} %bitcast.238) | data formatting | bytes 2359296 | tf_op jit(solution)/shard_map/reshape.7
  389.5 12.5 %fusion.57 = f32[48,4,2,32,2,32]{5,3,4,2,1,0:T(8,128)} fusion(bf16[48,48,2,4,32,1]{1,4,5,2,3,0:T(8,128)(2,1)} %copy.306, bf16[48,48,2,4,32,1]{1,4,2,5,3,0:T(8,128)(2,1)} %copy.303), kind=kOutput, calls=%fused_computation.98 | convolution fusion | flops 75497472 | bytes 5505024 | tf_op jit(solution)/shard_map/slmpgi,slmqgo->lgpiqo/dot_general | solution.py:111
  403.7 4.3 all-to-all-start.11
  408.0 7.5 %fusion.3 = (bf16[48,4,1,32,1,32]{5,3,4,2,1,0:T(8,128)(2,1)}, bf16[48,4,1,32,1,32]{5,3,4,2,1,0:T(8,128)(2,1)S(1)}) fusion(f32[48,4,2,32,2,32]{5,3,4,2,1,0:T(8,128)} %fusion.57), kind=kLoop, calls=%fused_computation.9 | loop fusion | flops 786432 | bytes 3932160 | tf_op jit(solution)/shard_map/convert.3
  415.6 2.9 reshape.378
  418.6 1.5 reshape.379
  422.1 290.2 %all-reduce.2.cloned.1.call-done = bf16[48,2,4,1024]{3,0,2,1:T(8,128)(2,1)} async-done(((bf16[48,2,4,1024]{3,0,2,1:T(8,128)(2,1)}), bf16[48,2,4,1024]{3,0,2,1:T(8,128)(2,1)}) %all-reduce.2.cloned.1.call-update) | async-done | bytes 786448 | tf_op jit(solution)/shard_map/psum | solution.py:117
  712.4 2.9 copy.299
  715.3 1.5 copy.293
  716.9 2.1 fusion.5
  (62 shorter events, 16.7 us)
Async XLA Ops:
  7.2 12.2 %copy-start = (bf16[1,6,768,128]{3,2,1,0:T(8,128)(2,1)S(1)}, bf16[1,6,768,128]{3,2,1,0:T(8,128)(2,1)}, u32[]{:S(2)}) copy-start(bf16[1,6,768,128]{3,2,1,0:T(8,128)(2,1)} %param.5) | copy-start | bytes 3538948
  50.4 21.1 %all-to-all-start.1 = ((bf16[8,1,48,12,128]{4,2,3,1,0:T(8,128)(2,1)}), bf16[8,1,48,12,128]{4,2,3,1,0:T(8,128)(2,1)S(1)}, u32[]{:S(2)}, u32[]{:S(2)}) async-start(bf16[8,1,48,12,128]{4,2,3,1,0:T(8,128)(2,1)} %copy.254), calls=%async_computation.1 | async-start | bytes 2359296 | tf_op jit(solution)/shard_map/all_to_all | solution.py:62
  85.3 6.4 copy-start.3
  85.3 30.9 %all-to-all-start.2 = ((bf16[1,384,12,128]{3,2,0,1:T(8,128)(2,1)}), bf16[1,384,12,128]{3,2,0,1:T(8,128)(2,1)}, u32[]{:S(2)}, u32[]{:S(2)}) async-start(bf16[1,384,12,128]{3,2,0,1:T(8,128)(2,1)} %copy.257), calls=%async_computation.2 | async-start | bytes 3145728 | tf_op jit(solution)/shard_map/all_to_all | solution.py:81
  204.7 21.6 %all-to-all-start.5 = ((bf16[1,48,96,128]{3,2,0,1:T(8,128)(2,1)}), bf16[1,48,96,128]{3,2,0,1:T(8,128)(2,1)}, u32[]{:S(2)}, u32[]{:S(2)}) async-start(bf16[1,48,96,128]{3,2,0,1:T(8,128)(2,1)} %copy.269), calls=%async_computation.5 | async-start | bytes 2359296 | tf_op jit(solution)/shard_map/all_to_all | solution.py:90
  291.8 23.0 %all-to-all-start.8 = ((bf16[1,384,12,128]{3,2,0,1:T(8,128)(2,1)}), bf16[1,384,12,128]{3,2,0,1:T(8,128)(2,1)S(1)}, u32[]{:S(2)}, u32[]{:S(2)}) async-start(bf16[1,384,12,128]{3,2,0,1:T(8,128)(2,1)} %copy.280), calls=%async_computation.8 | async-start | bytes 3145728 | tf_op jit(solution)/shard_map/all_to_all | solution.py:81
  375.9 26.1 %all-to-all-start.10 = ((bf16[1,384,12,128]{3,2,0,1:T(8,128)(2,1)}), bf16[1,384,12,128]{3,2,0,1:T(8,128)(2,1)S(1)}, u32[]{:S(2)}, u32[]{:S(2)}) async-start(bf16[1,384,12,128]{3,2,0,1:T(8,128)(2,1)} %copy.289), calls=%async_computation.10 | async-start | bytes 3145728 | tf_op jit(solution)/shard_map/all_to_all | solution.py:91
  403.7 311.5 %all-to-all-start.11 = ((bf16[1,48,96,128]{3,2,0,1:T(8,128)(2,1)}), bf16[1,48,96,128]{3,2,0,1:T(8,128)(2,1)}, u32[]{:S(2)}, u32[]{:S(2)}) async-start(bf16[1,48,96,128]{3,2,0,1:T(8,128)(2,1)} %copy.292), calls=%async_computation.11 | async-start | bytes 2359296 | tf_op jit(solution)/shard_map/all_to_all | solution.py:90
  408.0 304.4 %all-reduce.2.cloned.1.call-start = ((), (), s32[]{:S(2)}) async-start(), calls=%async_computation.12 | async-start | bytes 1572864 | tf_op jit(solution)/shard_map/psum | solution.py:117
  420.1 1.6 copy-start.2
  715.3 1.6 copy-start.4
  716.9 2.1 copy-start.1
Sparse Core Ops, SparseCore 0:
  421.3 290.9 all-reduce.1
